TPU v7x, 512 devices: a whole 4x4x16 slice. The times are simulated.
512 devices in a mesh: heads: 8 (over y, core), seq: 64 (over z, x).
Axes of the slice: x: 4, y: 4, z: 16, core: 2. Of those that a mesh axis runs over, the one named last changes fastest.
Arguments:
- query_proj: bfloat16 [8192, 4096], P('seq', 'heads'), may hold values from -6 to 6
- key_proj: bfloat16 [8192, 4096], P('seq', 'heads'), may hold values from -6 to 6
- value_proj: bfloat16 [8192, 4096], P('seq', 'heads'), may hold values from -6 to 6
- gate_proj: bfloat16 [8192, 4096], P('seq', 'heads'), may hold values from -6 to 6
- write_rate: float32 [32, 8192], P('heads', 'seq'), may hold values from 0 to 1
- log_decay: float32 [32, 8192], P('heads', 'seq'), may hold values from -1 to 0
- doc_start: int32 [8192], P('seq'), may hold values from 0 to 1, as said below
- norm_gain: float32 [128], replicated, may hold values from 0.5 to 1.5
- out_weight: bfloat16 [4096, 4096], P('heads', 'seq'), may hold values from -0.09375 to 0.09375
Outputs:
- layer_out: bfloat16 [8192, 4096], P('seq', 'heads')
Inputs may be any that keep to these rules, and one draw needn't show every extreme that they name: `doc_start`: exactly two entries are 1: one in the first half of the sequence (never token 0) and one in the second half.
All inputs are finite; a program needn't handle non-finite values.
Results may differ from a plain program's by a relative error of at most 0.017.
Values may be sent and summed in bfloat16 or wider, within the bound.
No kernel may reach another device: no remote copies, remote signals or barrier semaphores. Data moves between devices by JAX's collectives and lax.ppermute only.
A program may use at most 128 MiB of HBM per device.

v0:
```python
import jax
import jax.numpy as jnp
from jax import lax
from jax.sharding import Mesh
from jax.sharding import PartitionSpec as P

STRETCH = 64
SEQ_MINOR = 4
precise = lax.Precision.HIGHEST
epsilon = 1e-06


def unit_rows(block):
    return block / jnp.sqrt(jnp.sum(block * block, axis=-1, keepdims=True) + epsilon)


def triangular_inverse_below(system, right_side):
    return jax.scipy.linalg.solve_triangular(system, right_side, lower=True, unit_diagonal=True)


def matrix_product(left_side, right_side):
    return jnp.einsum("...de,...ef->...df", left_side, right_side, precision=precise)


def stretch_terms(queries, keys_normed, values_in, rates, decays, resets):
    length = queries.shape[-2]
    value_width = values_in.shape[-1]
    cumulated = jnp.cumsum(decays, axis=-1)
    seen = jnp.cumsum(resets, axis=-1)
    row_index = lax.broadcasted_iota(jnp.int32, (length, length), 0)
    col_index = lax.broadcasted_iota(jnp.int32, (length, length), 1)
    same_span = (seen[..., :, None] == seen[..., None, :]) & (row_index >= col_index)
    log_gap = jnp.where(same_span, cumulated[..., :, None] - cumulated[..., None, :], 0.0)
    pair_decay = jnp.where(same_span, jnp.exp(log_gap), 0.0)
    head_decay = jnp.exp(cumulated) * (seen == 0).astype(jnp.float32)
    tail_decay = jnp.exp(cumulated[..., -1:] - cumulated) * (seen[..., -1:] == seen).astype(
        jnp.float32
    )
    key_gram = jnp.einsum("...cd,...md->...cm", keys_normed, keys_normed, precision=precise)
    strict_part = jnp.where(row_index > col_index, rates[..., :, None] * pair_decay * key_gram, 0.0)
    system = strict_part + jnp.eye(length, dtype=jnp.float32)
    both_sides = jnp.concatenate(
        [rates[..., None] * values_in, (rates * head_decay)[..., None] * keys_normed], axis=-1
    )
    solved = triangular_inverse_below(system, both_sides)
    pseudo_values = solved[..., :value_width]
    key_weights = solved[..., value_width:]
    scores = pair_decay * jnp.einsum("...cd,...md->...cm", queries, keys_normed, precision=precise)
    query_state = head_decay[..., None] * queries - jnp.einsum(
        "...cm,...md->...cd", scores, key_weights, precision=precise
    )
    local_out = jnp.einsum("...cm,...md->...cd", scores, pseudo_values, precision=precise)
    identity = jnp.eye(keys_normed.shape[-1], dtype=jnp.float32)
    transit = head_decay[..., -1][..., None, None] * identity - jnp.einsum(
        "...cd,...ce->...de", keys_normed, tail_decay[..., None] * key_weights, precision=precise
    )
    written = jnp.einsum(
        "...cd,...ce->...de", keys_normed, tail_decay[..., None] * pseudo_values, precision=precise
    )
    return (query_state, local_out, transit, written)


def gated_norm(core_out, gate_block, gain):
    scale = lax.rsqrt(jnp.mean(core_out * core_out, axis=-1, keepdims=True) + epsilon)
    gate_float = gate_block.astype(jnp.float32)
    return (core_out * scale * gain * jax.nn.silu(gate_float)).astype(jnp.bfloat16)


def shift_down(array, step, fill):
    head = jnp.broadcast_to(fill, (step,) + array.shape[1:]).astype(array.dtype)
    return jnp.concatenate([head, array[:-step]], axis=0)


def on_device(
    query_proj,
    key_proj,
    value_proj,
    gate_proj,
    write_rate,
    log_decay,
    doc_start,
    norm_gain,
    out_weight,
    minor,
    major,
):
    head_count = write_rate.shape[0]
    key_width = query_proj.shape[1] // head_count
    value_width = value_proj.shape[1] // head_count

    def spread(array):
        return lax.all_to_all(array, "x", 1, 0, tiled=True)

    query_here = spread(query_proj)
    key_here = spread(key_proj)
    value_here = spread(value_proj)
    gate_here = spread(gate_proj)
    rates_here = lax.all_to_all(write_rate, "x", 0, 1, tiled=True)
    decays_here = lax.all_to_all(log_decay, "x", 0, 1, tiled=True)
    resets_here = lax.all_gather(doc_start, "x", tiled=True)
    tok_rows = query_here.shape[0]
    local_heads = head_count // minor
    blocks = tok_rows // STRETCH

    def stretch_major(array, width):
        return array.reshape(blocks, STRETCH, local_heads, width).transpose(0, 2, 1, 3)

    queries = unit_rows(stretch_major(query_here, key_width).astype(jnp.float32))
    keys_normed = unit_rows(stretch_major(key_here, key_width).astype(jnp.float32))
    values_in = stretch_major(value_here, value_width).astype(jnp.float32)
    rates = rates_here.reshape(local_heads, blocks, STRETCH).transpose(1, 0, 2)
    decays = decays_here.reshape(local_heads, blocks, STRETCH).transpose(1, 0, 2)
    resets = resets_here.reshape(blocks, 1, STRETCH)
    query_state, local_out, transit, written = stretch_terms(
        queries, keys_normed, values_in, rates, decays, resets
    )
    identity = jnp.eye(key_width, dtype=jnp.float32)
    reach, saved = (transit, written)
    step = 1
    while step < blocks:
        earlier_reach = shift_down(reach, step, identity)
        earlier_saved = shift_down(saved, step, 0.0)
        saved = matrix_product(reach, earlier_saved) + saved
        reach = matrix_product(reach, earlier_reach)
        step *= 2
    place = lax.axis_index("z")
    group_reach, group_saved = (reach[-1], saved[-1])
    step = 1
    while step < major:
        pairs = [(i, i + step) for i in range(major - step)]
        if 2 * step < major:
            got = lax.ppermute(jnp.stack([group_reach, group_saved]), "z", pairs)
            got_reach, got_saved = (got[0], got[1])
            new_saved = matrix_product(group_reach, got_saved) + group_saved
            group_reach = jnp.where(
                place >= step, matrix_product(group_reach, got_reach), group_reach
            )
        else:
            got_saved = lax.ppermute(group_saved, "z", pairs)
            new_saved = matrix_product(group_reach, got_saved) + group_saved
        group_saved = new_saved
        step *= 2
    incoming = lax.ppermute(group_saved, "z", [(i, i + 1) for i in range(major - 1)])
    entry_reach = shift_down(reach, 1, identity)
    entry_saved = shift_down(saved, 1, 0.0)
    entry_state = matrix_product(entry_reach, incoming[None]) + entry_saved
    core_out = (
        jnp.einsum("bhcd,bhde->bhce", query_state, entry_state, precision=precise) + local_out
    )
    core_tokens = core_out.transpose(0, 2, 1, 3).reshape(tok_rows, local_heads, value_width)
    normed = gated_norm(
        core_tokens, gate_here.reshape(tok_rows, local_heads, value_width), norm_gain
    )
    normed = normed.reshape(tok_rows, local_heads * value_width)
    normed = lax.all_to_all(normed, "x", 0, 1, tiled=True)
    partial_value = jnp.dot(
        normed,
        lax.all_gather(out_weight, ("z", "x"), axis=1, tiled=True),
        preferred_element_type=jnp.float32,
    )
    return lax.psum_scatter(
        partial_value.astype(jnp.bfloat16), "heads", scatter_dimension=1, tiled=True
    )


def solution(mesh):
    heads_size, seq_size = mesh.devices.shape
    minor = SEQ_MINOR
    major = seq_size // minor
    split_mesh = Mesh(mesh.devices.reshape(heads_size, major, minor), ("heads", "z", "x"))
    seq = ("z", "x")
    placed = (
        P(seq, "heads"),
        P(seq, "heads"),
        P(seq, "heads"),
        P(seq, "heads"),
        P("heads", seq),
        P("heads", seq),
        P(seq),
        P(),
        P("heads", seq),
    )

    def body(*arrays):
        return on_device(*arrays, minor=minor, major=major)

    return jax.shard_map(
        body, mesh=split_mesh, in_specs=placed, out_specs=P(seq, "heads"), check_vma=False
    )
```

profile of v0, /device:TPU:4, one launch (start us, length us, event | category | flops | bytes accessed | tf_op | source)
XLA Modules:
  0.0 234.6 jit_solution(6820988842869189103)
XLA Ops:
  6.5 9.2 %all-to-all-start = ((f32[4,1,128]{2,1,0:T(1,128)}), f32[4,1,128]{2,1,0:T(1,128)S(1)}, u32[]{:S(2)}, u32[]{:S(2)}) async-start(f32[4,1,128]{2,1,0:T(1,128)} %bitcast.231), calls=%async_computation | async-start | bytes 4096 | tf_op jit(solution)/shard_map/all_to_all | solution.py:99
  15.7 0.7 all-gather.3.cloned.1.call-update
  17.2 7.7 %all-gather = s32[4,1,128]{2,1,0:T(1,128)S(1)} all-gather(s32[1,1,128]{2,1,0:T(1,128)} %bitcast.233), channel_id=1, replica_groups=mesh['heads'=8,'z'=16,'x'=4] {'x'}, dimensions={0}, use_global_device_ids=true | all-gather | bytes 2560 | tf_op jit(solution)/shard_map/all_gather | solution.py:100
  26.4 1.6 copy_bitcast_fusion
  28.2 1.0 copy.59
  29.2 0.8 copy.60
  29.9 1.7 copy.69
  31.6 5.9 %all-to-all-start.3 = ((f32[4,1,128]{2,1,0:T(1,128)}), f32[4,1,128]{2,1,0:T(1,128)S(1)}, u32[]{:S(2)}, u32[]{:S(2)}) async-start(f32[4,1,128]{2,1,0:T(1,128)} %bitcast.232), calls=%async_computation.3 | async-start | bytes 4096 | tf_op jit(solution)/shard_map/all_to_all | solution.py:98
  39.1 1.3 all-to-all-done.3
  40.4 5.7 %all-to-all-start.2 = ((bf16[128,4,128]{2,0,1:T(8,128)(2,1)}), bf16[128,4,128]{2,0,1:T(8,128)(2,1)S(1)}, u32[]{:S(2)}, u32[]{:S(2)}) async-start(bf16[128,4,128]{2,0,1:T(8,128)(2,1)} %copy_bitcast_fusion.1), calls=%async_computation.2 | async-start | bytes 262144 | tf_op jit(solution)/shard_map/all_to_all | solution.py:92
  46.9 2.4 %all-to-all-done.2 = bf16[128,4,128]{2,0,1:T(8,128)(2,1)S(1)} async-done(((bf16[128,4,128]{2,0,1:T(8,128)(2,1)}), bf16[128,4,128]{2,0,1:T(8,128)(2,1)S(1)}, u32[]{:S(2)}, u32[]{:S(2)}) %all-to-all-start.2) | async-done | bytes 131104 | tf_op jit(solution)/shard_map/all_to_all | solution.py:92
  49.3 6.0 %all-to-all-start.4 = ((bf16[128,4,128]{2,0,1:T(8,128)(2,1)}), bf16[128,4,128]{2,0,1:T(8,128)(2,1)S(1)}, u32[]{:S(2)}, u32[]{:S(2)}) async-start(bf16[128,4,128]{2,0,1:T(8,128)(2,1)} %copy_bitcast_fusion), calls=%async_computation.4 | async-start | bytes 262144 | tf_op jit(solution)/shard_map/all_to_all | solution.py:92
  55.6 0.7 fusion.6
  56.3 39.3 %custom-call.4 = f32[8,1,64,64]{2,3,1,0:T(8,128)S(1)} custom-call(f32[8,1,64,64]{3,2,1,0:T(8,128)S(1)} %fusion.6), custom_call_target="InvertDiagBlocksLowerTriangular" | custom-call | tf_op jit(solution)/shard_map/jit(_solve_triangular)/vmap()/triangular_solve | solution.py:18
  95.6 4.8 %all-to-all-start.1 = ((bf16[128,4,128]{2,0,1:T(8,128)(2,1)}), bf16[128,4,128]{2,0,1:T(8,128)(2,1)S(1)}, u32[]{:S(2)}, u32[]{:S(2)}) async-start(bf16[128,4,128]{2,0,1:T(8,128)(2,1)} %copy.60), calls=%async_computation.1 | async-start | bytes 262144 | tf_op jit(solution)/shard_map/all_to_all | solution.py:92
  101.5 1.2 fusion.38
  102.7 1.2 convolution_subtract_fusion
  104.6 0.7 fusion.13
  108.0 1.3 collective-permute-start
  109.3 4.8 %all-to-all-start.5 = ((bf16[128,4,128]{0,2,1:T(8,128)(2,1)}), bf16[128,4,128]{0,2,1:T(8,128)(2,1)S(1)}, u32[]{:S(2)}, u32[]{:S(2)}) async-start(bf16[128,4,128]{0,2,1:T(8,128)(2,1)} %bitcast.67), calls=%async_computation.5 | async-start | bytes 262144 | tf_op jit(solution)/shard_map/all_to_all | solution.py:92
  114.4 0.7 convolution_multiply_fusion.1
  115.5 3.6 %collective-permute-start.1 = (f32[2,1,128,128]{3,2,1,0:T(8,128)S(1)}, f32[2,1,128,128]{3,2,1,0:T(8,128)S(1)}, u32[]{:S(2)}, u32[]{:S(2)}) collective-permute-start(f32[2,1,128,128]{3,2,1,0:T(8,128)S(1)} %pad_maximum_fusion.3), channel_id=1, source_target_pairs={{0,8},{4,12},{8,16},{12,20},{16,24},{20,28},{24,32},{28,36},{32,40... | collective-permute-start | bytes 393224 | tf_op jit(solution)/shard_map/ppermute | solution.py:132
  119.6 2.2 collective-permute-done.1
  122.3 12.9 %collective-permute-start.2 = (f32[2,1,128,128]{3,2,1,0:T(8,128)S(1)}, f32[2,1,128,128]{3,2,1,0:T(8,128)S(1)}, u32[]{:S(2)}, u32[]{:S(2)}) collective-permute-start(f32[2,1,128,128]{3,2,1,0:T(8,128)S(1)} %pad_maximum_fusion.4), channel_id=1, source_target_pairs={{0,16},{4,20},{8,24},{12,28},{16,32},{20,36},{24,40},{28,44},{32,4... | collective-permute-start | bytes 393224 | tf_op jit(solution)/shard_map/ppermute | solution.py:132
  135.3 3.5 %collective-permute-done.2 = f32[2,1,128,128]{3,2,1,0:T(8,128)S(1)} collective-permute-done((f32[2,1,128,128]{3,2,1,0:T(8,128)S(1)}, f32[2,1,128,128]{3,2,1,0:T(8,128)S(1)}, u32[]{:S(2)}, u32[]{:S(2)}) %collective-permute-start.2) | collective-permute-done | bytes 131104 | tf_op jit(solution)/shard_map/ppermute | solution.py:132
  139.0 21.5 %collective-permute-start.3 = (f32[1,128,128]{2,1,0:T(8,128)S(1)}, f32[1,128,128]{2,1,0:T(8,128)S(1)}, u32[]{:S(2)}, u32[]{:S(2)}) collective-permute-start(f32[1,128,128]{2,1,0:T(8,128)S(1)} %bitcast.226), channel_id=1, source_target_pairs={{0,32},{4,36},{8,40},{12,44},{16,48},{20,52},{24,56},{28,60},{1,33... | collective-permute-start | bytes 196616 | tf_op jit(solution)/shard_map/ppermute | solution.py:139
  160.7 1.9 collective-permute-done.3
  162.9 1.3 collective-permute-start.4
  164.2 1.8 collective-permute-done.4
  168.1 10.0 %all_to_all.94 = bf16[4,128,128]{1,2,0:T(8,128)(2,1)S(1)} all-to-all(bf16[4,128,128]{1,2,0:T(8,128)(2,1)S(1)} %fusion.45), channel_id=1, replica_groups=mesh['heads'=8,'z'=16,'x'=4] {'x'}, dimensions={0} | all-to-all | bytes 262144 | tf_op jit(solution)/shard_map/all_to_all | solution.py:155
  178.1 4.7 %convolution_convert_fusion = bf16[128,4096]{1,0:T(8,128)(2,1)} fusion(bf16[128,512]{0,1:T(8,128)(2,1)S(1)} %bitcast.223, bf16[512,4096]{0,1:T(8,128)(2,1)} %all-gather.3.cloned.1.call-done), kind=kOutput, calls=%fused_computation | convolution fusion | flops 537395200 | bytes 5373952 | tf_op jit(solution)/shard_map/dot_general | solution.py:156
  182.8 45.0 %reduce-scatter.2.cloned.1.call-done = bf16[128,512]{1,0:T(8,128)(2,1)} async-done(((bf16[128,4096]{1,0:T(8,128)(2,1)}), bf16[128,512]{1,0:T(8,128)(2,1)}) %reduce-scatter.2.cloned.1.call-update) | async-done | bytes 131088 | tf_op jit(solution)/shard_map/reduce_scatter | solution.py:161
  (82 shorter events, 13.8 us)
Async XLA Ops:
  6.5 10.0 %copy-start = (bf16[128,512]{1,0:T(8,128)(2,1)S(1)}, bf16[128,512]{1,0:T(8,128)(2,1)}, u32[]{:S(2)}) copy-start(bf16[128,512]{1,0:T(8,128)(2,1)} %param.10) | copy-start | bytes 393220
  6.5 25.1 %all-to-all-start = ((f32[4,1,128]{2,1,0:T(1,128)}), f32[4,1,128]{2,1,0:T(1,128)S(1)}, u32[]{:S(2)}, u32[]{:S(2)}) async-start(f32[4,1,128]{2,1,0:T(1,128)} %bitcast.231), calls=%async_computation | async-start | bytes 4096 | tf_op jit(solution)/shard_map/all_to_all | solution.py:99
  15.7 162.4 %all-gather.3.cloned.1.call-start = ((), (), s32[]{:S(2)}) async-start(), calls=%async_computation.8 | async-start | bytes 4259840 | tf_op jit(solution)/shard_map/all_gather | solution.py:158
  31.6 8.8 %all-to-all-start.3 = ((f32[4,1,128]{2,1,0:T(1,128)}), f32[4,1,128]{2,1,0:T(1,128)S(1)}, u32[]{:S(2)}, u32[]{:S(2)}) async-start(f32[4,1,128]{2,1,0:T(1,128)} %bitcast.232), calls=%async_computation.3 | async-start | bytes 4096 | tf_op jit(solution)/shard_map/all_to_all | solution.py:98
  40.4 8.9 %all-to-all-start.2 = ((bf16[128,4,128]{2,0,1:T(8,128)(2,1)}), bf16[128,4,128]{2,0,1:T(8,128)(2,1)S(1)}, u32[]{:S(2)}, u32[]{:S(2)}) async-start(bf16[128,4,128]{2,0,1:T(8,128)(2,1)} %copy_bitcast_fusion.1), calls=%async_computation.2 | async-start | bytes 262144 | tf_op jit(solution)/shard_map/all_to_all | solution.py:92
  49.3 46.3 %all-to-all-start.4 = ((bf16[128,4,128]{2,0,1:T(8,128)(2,1)}), bf16[128,4,128]{2,0,1:T(8,128)(2,1)S(1)}, u32[]{:S(2)}, u32[]{:S(2)}) async-start(bf16[128,4,128]{2,0,1:T(8,128)(2,1)} %copy_bitcast_fusion), calls=%async_computation.4 | async-start | bytes 262144 | tf_op jit(solution)/shard_map/all_to_all | solution.py:92
  95.6 13.7 %all-to-all-start.1 = ((bf16[128,4,128]{2,0,1:T(8,128)(2,1)}), bf16[128,4,128]{2,0,1:T(8,128)(2,1)S(1)}, u32[]{:S(2)}, u32[]{:S(2)}) async-start(bf16[128,4,128]{2,0,1:T(8,128)(2,1)} %copy.60), calls=%async_computation.1 | async-start | bytes 262144 | tf_op jit(solution)/shard_map/all_to_all | solution.py:92
  108.0 7.1 %collective-permute-start = (f32[2,1,128,128]{3,2,1,0:T(8,128)S(1)}, f32[2,1,128,128]{3,2,1,0:T(8,128)S(1)}, u32[]{:S(2)}, u32[]{:S(2)}) collective-permute-start(f32[2,1,128,128]{3,2,1,0:T(8,128)S(1)} %pad_maximum_fusion.2), channel_id=1, source_target_pairs={{0,4},{4,8},{8,12},{12,16},{16,20},{20,24},{24,28},{28,32},{32,36}... | collective-permute-start | bytes 393224 | tf_op jit(solution)/shard_map/ppermute | solution.py:132
  109.3 58.6 %all-to-all-start.5 = ((bf16[128,4,128]{0,2,1:T(8,128)(2,1)}), bf16[128,4,128]{0,2,1:T(8,128)(2,1)S(1)}, u32[]{:S(2)}, u32[]{:S(2)}) async-start(bf16[128,4,128]{0,2,1:T(8,128)(2,1)} %bitcast.67), calls=%async_computation.5 | async-start | bytes 262144 | tf_op jit(solution)/shard_map/all_to_all | solution.py:92
  114.1 113.7 %reduce-scatter.2.cloned.1.call-start = ((), (), s32[]{:S(2)}) async-start(), calls=%async_computation.9 | async-start | bytes 1179648 | tf_op jit(solution)/shard_map/reduce_scatter | solution.py:161
  115.5 6.3 %collective-permute-start.1 = (f32[2,1,128,128]{3,2,1,0:T(8,128)S(1)}, f32[2,1,128,128]{3,2,1,0:T(8,128)S(1)}, u32[]{:S(2)}, u32[]{:S(2)}) collective-permute-start(f32[2,1,128,128]{3,2,1,0:T(8,128)S(1)} %pad_maximum_fusion.3), channel_id=1, source_target_pairs={{0,8},{4,12},{8,16},{12,20},{16,24},{20,28},{24,32},{28,36},{32,40... | collective-permute-start | bytes 393224 | tf_op jit(solution)/shard_map/ppermute | solution.py:132
  119.2 48.8 %copy-start.1 = (f32[128]{0:T(128)S(1)}, f32[128]{0:T(128)}, u32[]{:S(2)}) copy-start(f32[128]{0:T(128)} %param.16) | copy-start | bytes 1540
  122.3 16.5 %collective-permute-start.2 = (f32[2,1,128,128]{3,2,1,0:T(8,128)S(1)}, f32[2,1,128,128]{3,2,1,0:T(8,128)S(1)}, u32[]{:S(2)}, u32[]{:S(2)}) collective-permute-start(f32[2,1,128,128]{3,2,1,0:T(8,128)S(1)} %pad_maximum_fusion.4), channel_id=1, source_target_pairs={{0,16},{4,20},{8,24},{12,28},{16,32},{20,36},{24,40},{28,44},{32,4... | collective-permute-start | bytes 393224 | tf_op jit(solution)/shard_map/ppermute | solution.py:132
  139.0 23.7 %collective-permute-start.3 = (f32[1,128,128]{2,1,0:T(8,128)S(1)}, f32[1,128,128]{2,1,0:T(8,128)S(1)}, u32[]{:S(2)}, u32[]{:S(2)}) collective-permute-start(f32[1,128,128]{2,1,0:T(8,128)S(1)} %bitcast.226), channel_id=1, source_target_pairs={{0,32},{4,36},{8,40},{12,44},{16,48},{20,52},{24,56},{28,60},{1,33... | collective-permute-start | bytes 196616 | tf_op jit(solution)/shard_map/ppermute | solution.py:139
  162.9 3.2 %collective-permute-start.4 = (f32[1,128,128]{2,1,0:T(8,128)S(1)}, f32[1,128,128]{2,1,0:T(8,128)S(1)}, u32[]{:S(2)}, u32[]{:S(2)}) collective-permute-start(f32[1,128,128]{2,1,0:T(8,128)S(1)} %fusion.7), channel_id=1, source_target_pairs={{0,4},{4,8},{8,12},{12,16},{16,20},{20,24},{24,28},{28,32},{32,36}... | collective-permute-start | bytes 196616 | tf_op jit(solution)/shard_map/ppermute | solution.py:143
Sparse Core Ops, SparseCore 0:
  19.4 151.3 all-gather.2
  182.9 44.7 reduce-scatter.1
where the time goes:
time: 235 us
  starting transfers between devices  77 us (33%)
  waiting for transfers between devices  58.9 us (25%)
  other arithmetic  42.6 us (18%)
  blocking collectives  17.7 us (8%)
  matrix products  16.4 us (7%)
  between operations  13.9 us (6%)
  local copies, waits for them, and re-layouts  8.12 us (3%)
    reduce_scatter x1, waiting for transfers between devices, on_device(): lax.psum_scatter(partial_value.astype(jnp.bfloat16), 'heads', scatter_dim...  45 us
    another operation x2, other arithmetic, triangular_inverse_below(): jax.scipy.linalg.solve_triangular(system, right_side, lower=True, unit_di...  39.3 us
    ppermute x1, starting transfers between devices, on_device(): got_saved = lax.ppermute(group_saved, 'z', pairs)  21.5 us
    all_to_all x4, starting transfers between devices, spread(): return lax.all_to_all(array, 'x', 1, 0, tiled=True)  21.3 us
    ppermute x3, starting transfers between devices, on_device(): got = lax.ppermute(jnp.stack([group_reach, group_saved]), 'z', pairs)  17.9 us
    all_to_all x1, blocking collectives, on_device(): normed = lax.all_to_all(normed, 'x', 0, 1, tiled=True)  10 us
    all_to_all x1, starting transfers between devices, on_device(): decays_here = lax.all_to_all(log_decay, 'x', 0, 1, tiled=True)  9.17 us
    all_gather x1, blocking collectives, on_device(): resets_here = lax.all_gather(doc_start, 'x', tiled=True)  7.65 us
  transfers between devices with their start and end apart: 13, of which 7 were waited for; matrix products, arithmetic and copies ran while one was open for 27% of the time, Pallas kernels for 0%

commit v1 on v0

--- a/solution.py
+++ b/solution.py
@@ -97,7 +97,9 @@
     gate_here = spread(gate_proj)
     rates_here = lax.all_to_all(write_rate, "x", 0, 1, tiled=True)
     decays_here = lax.all_to_all(log_decay, "x", 0, 1, tiled=True)
-    resets_here = lax.all_gather(doc_start, "x", tiled=True)
+    resets_here = jnp.concatenate(
+        lax.all_to_all(jnp.stack([doc_start] * lax.axis_size("x")), "x", 0, 0), axis=0
+    )
     tok_rows = query_here.shape[0]
     local_heads = head_count // minor
     blocks = tok_rows // STRETCH

time: 235 us -> 232 us (0.987)
  the two profiles are of different devices: /device:TPU:4 before, /device:TPU:2 now
where the time goes in v1:
time: 232 us; the launch traced here: 231 us
  starting transfers between devices  81 us (35%)
  waiting for transfers between devices  59.7 us (26%)
  other arithmetic  42.8 us (18%)
  matrix products  16.4 us (7%)
  between operations  13.9 us (6%)
  local copies, waits for them, and re-layouts  9.43 us (4%)
  blocking collectives  8.28 us (4%)
    reduce_scatter x1, waiting for transfers between devices, on_device(): lax.psum_scatter(partial_value.astype(jnp.bfloat16), 'heads', scatter_dim...  42.9 us
    another operation x2, other arithmetic, triangular_inverse_below(): jax.scipy.linalg.solve_triangular(system, right_side, lower=True, unit_di...  39.3 us
    ppermute x1, starting transfers between devices, on_device(): got_saved = lax.ppermute(group_saved, 'z', pairs)  20 us
    all_to_all x4, starting transfers between devices, spread(): return lax.all_to_all(array, 'x', 1, 0, tiled=True)  19.1 us
    ppermute x3, starting transfers between devices, on_device(): got = lax.ppermute(jnp.stack([group_reach, group_saved]), 'z', pairs)  17.2 us
    all_to_all x1, starting transfers between devices, on_device(): decays_here = lax.all_to_all(log_decay, 'x', 0, 1, tiled=True)  9.2 us
    all_to_all x1, blocking collectives, on_device(): normed = lax.all_to_all(normed, 'x', 0, 1, tiled=True)  8.28 us
    ppermute x1, starting transfers between devices, on_device(): lax.ppermute(group_saved, 'z', [(i, i + 1) for i in range(major - 1)])  6.04 us
  transfers between devices with their start and end apart: 14, of which 8 were waited for; matrix products, arithmetic and copies ran while one was open for 28% of the time, Pallas kernels for 0%

profile of v1, /device:TPU:2, one launch (start us, length us, event | category | flops | bytes accessed | tf_op | source)
XLA Modules:
  0.0 231.5 jit_solution(4127435185701801845)
XLA Ops:
  6.5 9.2 %all-to-all-start.1 = ((f32[4,1,128]{2,1,0:T(1,128)}), f32[4,1,128]{2,1,0:T(1,128)S(1)}, u32[]{:S(2)}, u32[]{:S(2)}) async-start(f32[4,1,128]{2,1,0:T(1,128)} %bitcast.230), calls=%async_computation.1 | async-start | bytes 4096 | tf_op jit(solution)/shard_map/all_to_all | solution.py:99
  15.7 0.7 all-gather.2.cloned.1.call-update
  17.3 1.6 copy_bitcast_fusion
  19.5 1.2 stack.28
  20.7 4.6 %all-to-all-start = ((s32[4,1,128]{2,1,0:T(1,128)}), s32[4,1,128]{2,1,0:T(1,128)S(1)}, u32[]{:S(2)}, u32[]{:S(2)}) async-start(s32[4,1,128]{2,1,0:T(1,128)} %stack.28), calls=%async_computation | async-start | bytes 4096 | tf_op jit(solution)/shard_map/all_to_all | solution.py:101
  25.4 1.0 copy.59
  26.4 0.8 copy.60
  27.2 1.7 copy.69
  29.4 0.7 reduce.23
  30.2 4.8 %all-to-all-start.4 = ((f32[4,1,128]{2,1,0:T(1,128)}), f32[4,1,128]{2,1,0:T(1,128)S(1)}, u32[]{:S(2)}, u32[]{:S(2)}) async-start(f32[4,1,128]{2,1,0:T(1,128)} %bitcast.231), calls=%async_computation.4 | async-start | bytes 4096 | tf_op jit(solution)/shard_map/all_to_all | solution.py:98
  36.9 1.8 all-to-all-done.4
  38.7 4.7 %all-to-all-start.3 = ((bf16[128,4,128]{2,0,1:T(8,128)(2,1)}), bf16[128,4,128]{2,0,1:T(8,128)(2,1)S(1)}, u32[]{:S(2)}, u32[]{:S(2)}) async-start(bf16[128,4,128]{2,0,1:T(8,128)(2,1)} %copy_bitcast_fusion.1), calls=%async_computation.3 | async-start | bytes 262144 | tf_op jit(solution)/shard_map/all_to_all | solution.py:92
  44.5 4.1 %all-to-all-done.3 = bf16[128,4,128]{2,0,1:T(8,128)(2,1)S(1)} async-done(((bf16[128,4,128]{2,0,1:T(8,128)(2,1)}), bf16[128,4,128]{2,0,1:T(8,128)(2,1)S(1)}, u32[]{:S(2)}, u32[]{:S(2)}) %all-to-all-start.3) | async-done | bytes 131104 | tf_op jit(solution)/shard_map/all_to_all | solution.py:92
  48.6 4.7 %all-to-all-start.5 = ((bf16[128,4,128]{2,0,1:T(8,128)(2,1)}), bf16[128,4,128]{2,0,1:T(8,128)(2,1)S(1)}, u32[]{:S(2)}, u32[]{:S(2)}) async-start(bf16[128,4,128]{2,0,1:T(8,128)(2,1)} %copy_bitcast_fusion), calls=%async_computation.5 | async-start | bytes 262144 | tf_op jit(solution)/shard_map/all_to_all | solution.py:92
  53.6 0.7 fusion.6
  54.3 39.3 %custom-call.4 = f32[8,1,64,64]{2,3,1,0:T(8,128)S(1)} custom-call(f32[8,1,64,64]{3,2,1,0:T(8,128)S(1)} %fusion.6), custom_call_target="InvertDiagBlocksLowerTriangular" | custom-call | tf_op jit(solution)/shard_map/jit(_solve_triangular)/vmap()/triangular_solve | solution.py:18
  93.7 4.8 %all-to-all-start.2 = ((bf16[128,4,128]{2,0,1:T(8,128)(2,1)}), bf16[128,4,128]{2,0,1:T(8,128)(2,1)S(1)}, u32[]{:S(2)}, u32[]{:S(2)}) async-start(bf16[128,4,128]{2,0,1:T(8,128)(2,1)} %copy.60), calls=%async_computation.2 | async-start | bytes 262144 | tf_op jit(solution)/shard_map/all_to_all | solution.py:92
  99.5 1.2 fusion.38
  100.7 1.2 convolution_subtract_fusion
  106.0 1.3 collective-permute-start
  107.3 4.8 %all-to-all-start.6 = ((bf16[128,4,128]{0,2,1:T(8,128)(2,1)}), bf16[128,4,128]{0,2,1:T(8,128)(2,1)S(1)}, u32[]{:S(2)}, u32[]{:S(2)}) async-start(bf16[128,4,128]{0,2,1:T(8,128)(2,1)} %bitcast.66), calls=%async_computation.6 | async-start | bytes 262144 | tf_op jit(solution)/shard_map/all_to_all | solution.py:92
  113.6 3.2 %collective-permute-start.1 = (f32[2,1,128,128]{3,2,1,0:T(8,128)S(1)}, f32[2,1,128,128]{3,2,1,0:T(8,128)S(1)}, u32[]{:S(2)}, u32[]{:S(2)}) collective-permute-start(f32[2,1,128,128]{3,2,1,0:T(8,128)S(1)} %pad_maximum_fusion.3), channel_id=1, source_target_pairs={{0,8},{4,12},{8,16},{12,20},{16,24},{20,28},{24,32},{28,36},{32,40... | collective-permute-start | bytes 393224 | tf_op jit(solution)/shard_map/ppermute | solution.py:134
  117.2 2.2 collective-permute-done.1
  119.8 12.8 %collective-permute-start.2 = (f32[2,1,128,128]{3,2,1,0:T(8,128)S(1)}, f32[2,1,128,128]{3,2,1,0:T(8,128)S(1)}, u32[]{:S(2)}, u32[]{:S(2)}) collective-permute-start(f32[2,1,128,128]{3,2,1,0:T(8,128)S(1)} %pad_maximum_fusion.4), channel_id=1, source_target_pairs={{0,16},{4,20},{8,24},{12,28},{16,32},{20,36},{24,40},{28,44},{32,4... | collective-permute-start | bytes 393224 | tf_op jit(solution)/shard_map/ppermute | solution.py:134
  132.7 3.1 %collective-permute-done.2 = f32[2,1,128,128]{3,2,1,0:T(8,128)S(1)} collective-permute-done((f32[2,1,128,128]{3,2,1,0:T(8,128)S(1)}, f32[2,1,128,128]{3,2,1,0:T(8,128)S(1)}, u32[]{:S(2)}, u32[]{:S(2)}) %collective-permute-start.2) | collective-permute-done | bytes 131104 | tf_op jit(solution)/shard_map/ppermute | solution.py:134
  136.0 20.0 %collective-permute-start.3 = (f32[1,128,128]{2,1,0:T(8,128)S(1)}, f32[1,128,128]{2,1,0:T(8,128)S(1)}, u32[]{:S(2)}, u32[]{:S(2)}) collective-permute-start(f32[1,128,128]{2,1,0:T(8,128)S(1)} %bitcast.225), channel_id=1, source_target_pairs={{0,32},{4,36},{8,40},{12,44},{16,48},{20,52},{24,56},{28,60},{1,33... | collective-permute-start | bytes 196616 | tf_op jit(solution)/shard_map/ppermute | solution.py:141
  156.2 2.1 collective-permute-done.3
  158.6 6.0 %collective-permute-start.4 = (f32[1,128,128]{2,1,0:T(8,128)S(1)}, f32[1,128,128]{2,1,0:T(8,128)S(1)}, u32[]{:S(2)}, u32[]{:S(2)}) collective-permute-start(f32[1,128,128]{2,1,0:T(8,128)S(1)} %fusion.7), channel_id=1, source_target_pairs={{0,4},{4,8},{8,12},{12,16},{16,20},{20,24},{24,28},{28,32},{32,36}... | collective-permute-start | bytes 196616 | tf_op jit(solution)/shard_map/ppermute | solution.py:145
  164.7 2.1 collective-permute-done.4
  168.8 8.3 %all_to_all.100 = bf16[4,128,128]{1,2,0:T(8,128)(2,1)S(1)} all-to-all(bf16[4,128,128]{1,2,0:T(8,128)(2,1)S(1)} %fusion.45), channel_id=1, replica_groups=mesh['heads'=8,'z'=16,'x'=4] {'x'}, dimensions={0} | all-to-all | bytes 262144 | tf_op jit(solution)/shard_map/all_to_all | solution.py:157
  177.1 4.7 %convolution_convert_fusion = bf16[128,4096]{1,0:T(8,128)(2,1)} fusion(bf16[128,512]{0,1:T(8,128)(2,1)S(1)} %bitcast.222, bf16[512,4096]{0,1:T(8,128)(2,1)} %all-gather.2.cloned.1.call-done), kind=kOutput, calls=%fused_computation | convolution fusion | flops 537395200 | bytes 5373952 | tf_op jit(solution)/shard_map/dot_general | solution.py:158
  181.8 42.9 %reduce-scatter.2.cloned.1.call-done = bf16[128,512]{1,0:T(8,128)(2,1)} async-done(((bf16[128,4096]{1,0:T(8,128)(2,1)}), bf16[128,512]{1,0:T(8,128)(2,1)}) %reduce-scatter.2.cloned.1.call-update) | async-done | bytes 131088 | tf_op jit(solution)/shard_map/reduce_scatter | solution.py:163
  (84 shorter events, 15.3 us)
Async XLA Ops:
  6.5 10.0 %copy-start = (bf16[128,512]{1,0:T(8,128)(2,1)S(1)}, bf16[128,512]{1,0:T(8,128)(2,1)}, u32[]{:S(2)}) copy-start(bf16[128,512]{1,0:T(8,128)(2,1)} %param.10) | copy-start | bytes 393220
  6.5 13.0 %all-to-all-start.1 = ((f32[4,1,128]{2,1,0:T(1,128)}), f32[4,1,128]{2,1,0:T(1,128)S(1)}, u32[]{:S(2)}, u32[]{:S(2)}) async-start(f32[4,1,128]{2,1,0:T(1,128)} %bitcast.230), calls=%async_computation.1 | async-start | bytes 4096 | tf_op jit(solution)/shard_map/all_to_all | solution.py:99
  15.7 161.3 %all-gather.2.cloned.1.call-start = ((), (), s32[]{:S(2)}) async-start(), calls=%async_computation.9 | async-start | bytes 4259840 | tf_op jit(solution)/shard_map/all_gather | solution.py:160
  20.7 9.4 %all-to-all-start = ((s32[4,1,128]{2,1,0:T(1,128)}), s32[4,1,128]{2,1,0:T(1,128)S(1)}, u32[]{:S(2)}, u32[]{:S(2)}) async-start(s32[4,1,128]{2,1,0:T(1,128)} %stack.28), calls=%async_computation | async-start | bytes 4096 | tf_op jit(solution)/shard_map/all_to_all | solution.py:101
  30.2 8.6 %all-to-all-start.4 = ((f32[4,1,128]{2,1,0:T(1,128)}), f32[4,1,128]{2,1,0:T(1,128)S(1)}, u32[]{:S(2)}, u32[]{:S(2)}) async-start(f32[4,1,128]{2,1,0:T(1,128)} %bitcast.231), calls=%async_computation.4 | async-start | bytes 4096 | tf_op jit(solution)/shard_map/all_to_all | solution.py:98
  38.7 9.9 %all-to-all-start.3 = ((bf16[128,4,128]{2,0,1:T(8,128)(2,1)}), bf16[128,4,128]{2,0,1:T(8,128)(2,1)S(1)}, u32[]{:S(2)}, u32[]{:S(2)}) async-start(bf16[128,4,128]{2,0,1:T(8,128)(2,1)} %copy_bitcast_fusion.1), calls=%async_computation.3 | async-start | bytes 262144 | tf_op jit(solution)/shard_map/all_to_all | solution.py:92
  48.6 45.1 %all-to-all-start.5 = ((bf16[128,4,128]{2,0,1:T(8,128)(2,1)}), bf16[128,4,128]{2,0,1:T(8,128)(2,1)S(1)}, u32[]{:S(2)}, u32[]{:S(2)}) async-start(bf16[128,4,128]{2,0,1:T(8,128)(2,1)} %copy_bitcast_fusion), calls=%async_computation.5 | async-start | bytes 262144 | tf_op jit(solution)/shard_map/all_to_all | solution.py:92
  93.7 13.7 %all-to-all-start.2 = ((bf16[128,4,128]{2,0,1:T(8,128)(2,1)}), bf16[128,4,128]{2,0,1:T(8,128)(2,1)S(1)}, u32[]{:S(2)}, u32[]{:S(2)}) async-start(bf16[128,4,128]{2,0,1:T(8,128)(2,1)} %copy.60), calls=%async_computation.2 | async-start | bytes 262144 | tf_op jit(solution)/shard_map/all_to_all | solution.py:92
  106.0 7.1 %collective-permute-start = (f32[2,1,128,128]{3,2,1,0:T(8,128)S(1)}, f32[2,1,128,128]{3,2,1,0:T(8,128)S(1)}, u32[]{:S(2)}, u32[]{:S(2)}) collective-permute-start(f32[2,1,128,128]{3,2,1,0:T(8,128)S(1)} %pad_maximum_fusion.2), channel_id=1, source_target_pairs={{0,4},{4,8},{8,12},{12,16},{16,20},{20,24},{24,28},{28,32},{32,36}... | collective-permute-start | bytes 393224 | tf_op jit(solution)/shard_map/ppermute | solution.py:134
  107.3 61.3 %all-to-all-start.6 = ((bf16[128,4,128]{0,2,1:T(8,128)(2,1)}), bf16[128,4,128]{0,2,1:T(8,128)(2,1)S(1)}, u32[]{:S(2)}, u32[]{:S(2)}) async-start(bf16[128,4,128]{0,2,1:T(8,128)(2,1)} %bitcast.66), calls=%async_computation.6 | async-start | bytes 262144 | tf_op jit(solution)/shard_map/all_to_all | solution.py:92
  112.2 112.5 %reduce-scatter.2.cloned.1.call-start = ((), (), s32[]{:S(2)}) async-start(), calls=%async_computation.10 | async-start | bytes 1179648 | tf_op jit(solution)/shard_map/reduce_scatter | solution.py:163
  113.6 5.8 %collective-permute-start.1 = (f32[2,1,128,128]{3,2,1,0:T(8,128)S(1)}, f32[2,1,128,128]{3,2,1,0:T(8,128)S(1)}, u32[]{:S(2)}, u32[]{:S(2)}) collective-permute-start(f32[2,1,128,128]{3,2,1,0:T(8,128)S(1)} %pad_maximum_fusion.3), channel_id=1, source_target_pairs={{0,8},{4,12},{8,16},{12,20},{16,24},{20,28},{24,32},{28,36},{32,40... | collective-permute-start | bytes 393224 | tf_op jit(solution)/shard_map/ppermute | solution.py:134
  116.8 51.9 %copy-start.1 = (f32[128]{0:T(128)S(1)}, f32[128]{0:T(128)}, u32[]{:S(2)}) copy-start(f32[128]{0:T(128)} %param.16) | copy-start | bytes 1540
  119.8 15.9 %collective-permute-start.2 = (f32[2,1,128,128]{3,2,1,0:T(8,128)S(1)}, f32[2,1,128,128]{3,2,1,0:T(8,128)S(1)}, u32[]{:S(2)}, u32[]{:S(2)}) collective-permute-start(f32[2,1,128,128]{3,2,1,0:T(8,128)S(1)} %pad_maximum_fusion.4), channel_id=1, source_target_pairs={{0,16},{4,20},{8,24},{12,28},{16,32},{20,36},{24,40},{28,44},{32,4... | collective-permute-start | bytes 393224 | tf_op jit(solution)/shard_map/ppermute | solution.py:134
  136.0 22.4 %collective-permute-start.3 = (f32[1,128,128]{2,1,0:T(8,128)S(1)}, f32[1,128,128]{2,1,0:T(8,128)S(1)}, u32[]{:S(2)}, u32[]{:S(2)}) collective-permute-start(f32[1,128,128]{2,1,0:T(8,128)S(1)} %bitcast.225), channel_id=1, source_target_pairs={{0,32},{4,36},{8,40},{12,44},{16,48},{20,52},{24,56},{28,60},{1,33... | collective-permute-start | bytes 196616 | tf_op jit(solution)/shard_map/ppermute | solution.py:141
  158.6 8.2 %collective-permute-start.4 = (f32[1,128,128]{2,1,0:T(8,128)S(1)}, f32[1,128,128]{2,1,0:T(8,128)S(1)}, u32[]{:S(2)}, u32[]{:S(2)}) collective-permute-start(f32[1,128,128]{2,1,0:T(8,128)S(1)} %fusion.7), channel_id=1, source_target_pairs={{0,4},{4,8},{8,12},{12,16},{16,20},{20,24},{24,28},{28,32},{32,36}... | collective-permute-start | bytes 196616 | tf_op jit(solution)/shard_map/ppermute | solution.py:145
Sparse Core Ops, SparseCore 0:
  19.5 150.8 all-gather.1
  181.9 42.6 reduce-scatter.1
